TPU v7x, 512 devices: a whole 4x8x8 slice. The times are simulated.
512 devices in a mesh: dp: 16 (over z, core), expert: 32 (over x, y).
Axes of the slice: x: 4, y: 8, z: 8, core: 2. Of those that a mesh axis runs over, the one named last changes fastest.
Arguments:
- tokens: bfloat16 [65536, 1024], P(('dp', 'expert')), may hold values from -6 to 6
- expert_ids: int32 [65536, 8], P(('dp', 'expert')), may hold values from 0 to 63, all different within a row; in each aligned block of 128 rows (0 to 127, 128 to 255, ...) at most 17 rows name the same one
- gate_values: float32 [65536, 8], P(('dp', 'expert')), may hold values from 0.05 to 0.5
- w_gate: bfloat16 [64, 1024, 384], P('expert', 'dp'), may hold values from -0.1875 to 0.1875
- w_up: bfloat16 [64, 1024, 384], P('expert', 'dp'), may hold values from -0.1875 to 0.1875
- w_down: bfloat16 [64, 384, 1024], P('expert', 'dp'), may hold values from -0.3125 to 0.3125
- partner: int32 [512], replicated, may hold values from 0 to 511, as said below
Outputs:
- contrast_loss: float32 [], replicated
- token_grad: bfloat16 [65536, 1024], P(('dp', 'expert'))
- gate_grad: float32 [65536, 8], P(('dp', 'expert'))
Inputs may be any that keep to these rules, and one draw needn't show every extreme that they name: `expert_ids`: each row names 8 different experts. Among the 128 rows of one sequence no expert is named more than 17 times, and in every draw some sequence names some expert exactly 17 times. partner[i] differs from i.
All inputs are finite; a program needn't handle non-finite values.
Results may differ from a plain program's by a relative error of at most 0.014.
Values may be sent and summed in bfloat16 or wider, within the bound.
No kernel may reach another device: no remote copies, remote signals or barrier semaphores. Data moves between devices by JAX's collectives and lax.ppermute only.
A program may use at most 64 MiB of HBM per device.

v0:
```python
import jax
import jax.numpy as jnp
from jax import lax
from jax.sharding import PartitionSpec as P

score_scale = 20.0
highest = lax.Precision.HIGHEST


def silu_parts(pre_act):
    sigmoid_val = jax.nn.sigmoid(pre_act)
    return (pre_act * sigmoid_val, sigmoid_val * (1.0 + pre_act * (1.0 - sigmoid_val)))


def expert_forward(slot_piece, gate_full, up_full, down_full):
    pre_gate = jnp.einsum(
        "encd,edf->encf", slot_piece, gate_full, preferred_element_type=jnp.float32
    )
    pre_up = jnp.einsum("encd,edf->encf", slot_piece, up_full, preferred_element_type=jnp.float32)
    activated, derivative = silu_parts(pre_gate)
    hidden = (activated * pre_up).astype(jnp.bfloat16)
    expert_out = jnp.einsum(
        "encf,efd->encd", hidden, down_full, preferred_element_type=jnp.float32
    ).astype(jnp.bfloat16)
    return (expert_out, pre_gate, pre_up)


def on_device(tokens, expert_ids, gate_values, w_gate, w_up, w_down, partner):
    tok_rows, model_width = tokens.shape
    route_count = expert_ids.shape[1]
    local_experts = w_gate.shape[0]
    experts = lax.axis_size("expert") * local_experts
    capacity = tok_rows * route_count // experts + max(1, tok_rows * route_count // (16 * experts))
    slot_total = experts * capacity
    gate_full, up_full, down_full = (
        lax.all_gather(w_gate, "dp", axis=1, tiled=True),
        lax.all_gather(w_up, "dp", axis=1, tiled=True),
        lax.all_gather(w_down, "dp", axis=1, tiled=True),
    )
    expert_iota = jnp.arange(experts, dtype=jnp.int32)
    matches = expert_ids[:, :, None] == expert_iota
    chosen = jnp.sum(matches.astype(jnp.int32), axis=1, dtype=jnp.int32)
    chosen_gate = jnp.sum(jnp.where(matches, gate_values[:, :, None], 0.0), axis=1)
    before = jnp.cumsum(chosen, axis=0, dtype=jnp.int32) - chosen
    slot_rank = jnp.take_along_axis(before, expert_ids, axis=1)
    slot_row = (expert_ids * capacity + slot_rank).reshape(-1)
    slot_iota = jnp.arange(capacity, dtype=jnp.int32)
    onehot = (chosen.T[:, None, :] == 1) & (before.T[:, None, :] == slot_iota[None, :, None])
    placer = onehot.astype(jnp.bfloat16)
    slot_gate = jnp.sum(jnp.where(onehot, chosen_gate.T[:, None, :], 0.0), axis=2)
    outgoing = jnp.einsum("ect,td->ecd", placer, tokens, preferred_element_type=jnp.float32).astype(
        jnp.bfloat16
    )
    outgoing = outgoing.reshape(experts, 1, capacity, model_width)
    placer_flat = placer.reshape(slot_total, tok_rows)
    out_here, pre_gate, pre_up = expert_forward(
        lax.all_to_all(outgoing, "expert", split_axis=0, concat_axis=1, tiled=True),
        gate_full,
        up_full,
        down_full,
    )
    returned_out = lax.all_to_all(
        out_here, "expert", split_axis=1, concat_axis=0, tiled=True
    ).reshape(slot_total, model_width)
    weighted_sum = jnp.dot(
        slot_gate.reshape(slot_total), returned_out.astype(jnp.float32), precision=highest
    )
    pooled = jnp.mean(tokens.astype(jnp.float32), axis=0) + weighted_sum / tok_rows
    inv_rms = lax.rsqrt(jnp.mean(pooled * pooled) + 1e-06)
    embedding = (pooled * inv_rms).astype(jnp.bfloat16)[None, :]
    gathered = lax.all_gather(embedding, ("dp", "expert"), axis=0, tiled=True)
    batch_size = gathered.shape[0]
    own_index = lax.axis_index(("dp", "expert"))
    batch_iota = jnp.arange(batch_size, dtype=jnp.int32)
    scores = (
        score_scale
        / model_width
        * jnp.dot(gathered, embedding[0], preferred_element_type=jnp.float32)
    )
    others = batch_iota != own_index
    log_total = jnp.log(jnp.sum(jnp.where(others, jnp.exp(scores), 0.0)))
    own_partner = lax.dynamic_index_in_dim(partner, own_index, keepdims=False)
    partner_hit = (batch_iota == own_partner).astype(jnp.float32)
    weight = jnp.where(others, jnp.exp(scores - log_total), 0.0) - partner_hit
    all_embed = gathered.astype(jnp.float32)
    row_term = jnp.dot(weight, all_embed, precision=highest)
    all_totals = lax.all_gather(log_total[None], ("dp", "expert"), axis=0, tiled=True)
    column_weight = jnp.where(others, jnp.exp(scores - all_totals), 0.0) - (
        partner == own_index
    ).astype(jnp.float32)
    embed_grad = (
        score_scale
        / model_width
        * (row_term + jnp.dot(column_weight, all_embed, precision=highest))
    )
    partner_rows = jnp.take(gathered, partner, axis=0)
    partner_score = (
        score_scale
        / model_width
        * jnp.einsum("bd,bd->b", gathered, partner_rows, preferred_element_type=jnp.float32)
    )
    contrast_loss = jnp.mean(all_totals - partner_score)
    seq_grad = (
        inv_rms * embed_grad - inv_rms**3 * jnp.sum(pooled * embed_grad) / model_width * pooled
    )
    slot_dots = jnp.dot(returned_out.astype(jnp.float32), seq_grad, precision=highest)
    gate_grad = jnp.take(slot_dots, slot_row, axis=0).reshape(tok_rows, route_count)
    out_grad = (
        (slot_gate[:, :, None] * seq_grad)
        .astype(jnp.bfloat16)
        .reshape(experts, 1, capacity, model_width)
    )
    arrived = lax.all_to_all(out_grad, "expert", split_axis=0, concat_axis=1, tiled=True)
    hidden_grad = jnp.einsum(
        "encd,efd->encf", arrived, down_full, preferred_element_type=jnp.float32
    )
    activated, derivative = silu_parts(pre_gate)
    gate_side = (hidden_grad * pre_up * derivative).astype(jnp.bfloat16)
    up_side = (hidden_grad * activated).astype(jnp.bfloat16)
    route_here = jnp.einsum(
        "encf,edf->encd", gate_side, gate_full, preferred_element_type=jnp.float32
    )
    route_here = (
        route_here
        + jnp.einsum("encf,edf->encd", up_side, up_full, preferred_element_type=jnp.float32)
    ).astype(jnp.bfloat16)
    returned = lax.all_to_all(
        route_here, "expert", split_axis=1, concat_axis=0, tiled=True
    ).reshape(slot_total, model_width)
    route_sum = jnp.einsum("st,sd->td", placer_flat, returned, preferred_element_type=jnp.float32)
    token_grad = (seq_grad + route_sum).astype(jnp.bfloat16)
    return (contrast_loss, token_grad, gate_grad)


def solution(mesh):
    placed = (
        P(("dp", "expert"), None),
        P(("dp", "expert"), None),
        P(("dp", "expert"), None),
        P("expert", "dp", None),
        P("expert", "dp", None),
        P("expert", "dp", None),
        P(),
    )
    return jax.shard_map(
        on_device,
        mesh=mesh,
        in_specs=placed,
        out_specs=(P(), P(("dp", "expert"), None), P(("dp", "expert"), None)),
        check_vma=False,
    )
```

profile of v0, /device:TPU:16, one launch (start us, length us, event | category | flops | bytes accessed | tf_op | source)
XLA Modules:
  0.0 604.4 jit_solution(16274606224665401877)
XLA Ops:
  11.6 3.0 copy.118
  14.7 10.1 %all-to-all-start = ((bf16[64,1,17,1024]{3,2,1,0:T(8,128)(2,1)}), bf16[64,1,17,1024]{3,2,1,0:T(8,128)(2,1)S(1)}, u32[]{:S(2)}, u32[]{:S(2)}) async-start(bf16[64,1,17,1024]{3,2,1,0:T(8,128)(2,1)} %copy.118), calls=%async_computation | async-start | bytes 6291456 | tf_op jit(solution)/shard_map/all_to_all | solution.py:57
  25.5 31.7 %all-gather.6.cloned.1.call-done = bf16[2,1024,384]{2,1,0:T(8,128)(2,1)} async-done(((bf16[2,64,384]{2,1,0:T(8,128)(2,1)}), bf16[2,1024,384]{2,1,0:T(8,128)(2,1)}) %all-gather.6.cloned.1.call-update) | async-done | bytes 1572880 | tf_op jit(solution)/shard_map/all_gather | solution.py:36
  57.1 39.8 %all-to-all-done = bf16[64,1,17,1024]{3,2,1,0:T(8,128)(2,1)S(1)} async-done(((bf16[64,1,17,1024]{3,2,1,0:T(8,128)(2,1)}), bf16[64,1,17,1024]{3,2,1,0:T(8,128)(2,1)S(1)}, u32[]{:S(2)}, u32[]{:S(2)}) %all-to-all-start) | async-done | bytes 2228256 | tf_op jit(solution)/shard_map/all_to_all | solution.py:57
  96.9 4.3 fusion.5
  101.2 4.2 fusion.3
  105.4 37.3 %all-gather.10.cloned.1.call-done = bf16[2,384,1024]{2,1,0:T(8,128)(2,1)} async-done(((bf16[2,24,1024]{2,1,0:T(8,128)(2,1)}), bf16[2,384,1024]{2,1,0:T(8,128)(2,1)}) %all-gather.10.cloned.1.call-update) | async-done | bytes 1572880 | tf_op jit(solution)/shard_map/all_gather | solution.py:38
  142.7 3.8 convolution_convert_fusion
  146.5 3.7 copy.121
  150.2 10.0 %all-to-all-start.1 = ((bf16[2,32,17,1024]{3,0,2,1:T(2,128)(2,1)}), bf16[2,32,17,1024]{3,0,2,1:T(2,128)(2,1)S(1)}, u32[]{:S(2)}, u32[]{:S(2)}) async-start(bf16[2,32,17,1024]{3,0,2,1:T(2,128)(2,1)} %copy.121), calls=%async_computation.1 | async-start | bytes 4456448 | tf_op jit(solution)/shard_map/all_to_all | solution.py:62
  161.0 52.4 %all-to-all-done.1 = bf16[2,32,17,1024]{3,0,2,1:T(2,128)(2,1)S(1)} async-done(((bf16[2,32,17,1024]{3,0,2,1:T(2,128)(2,1)}), bf16[2,32,17,1024]{3,0,2,1:T(2,128)(2,1)S(1)}, u32[]{:S(2)}, u32[]{:S(2)}) %all-to-all-start.1) | async-done | bytes 2228256 | tf_op jit(solution)/shard_map/all_to_all | solution.py:62
  213.4 2.7 copy.122
  216.1 3.0 reshape.128
  225.1 102.9 %all-gather.12.cloned.1.call-done = bf16[524288]{0:T(1024)(128)(2,1)} async-done(((bf16[1024]{0:T(1024)(128)(2,1)}), bf16[524288]{0:T(1024)(128)(2,1)}) %all-gather.12.cloned.1.call-update) | async-done | bytes 1048592 | tf_op jit(solution)/shard_map/all_gather | solution.py:71
  333.8 97.6 %all-reduce = f32[512]{0:T(512)} all-reduce(f32[512]{0:T(512)} %dynamic-update-slice), channel_id=1, replica_groups=mesh['dp'=16,'expert'=32] {'dp','expert'}, use_global_device_ids=true, to_apply=%add | all-reduce | flops 512 | bytes 4096
  431.4 2.9 gather_fusion
  441.6 79.0 %all_to_all.66 = bf16[64,1,17,1024]{3,2,1,0:T(8,128)(2,1)S(1)} all-to-all(bf16[64,1,17,1024]{3,2,1,0:T(8,128)(2,1)S(1)} %multiply_convert_fusion), channel_id=1, replica_groups=mesh['dp'=16,'expert'=32] {'expert'}, dimensions={0} | all-to-all | bytes 4456448 | tf_op jit(solution)/shard_map/all_to_all | solution.py:113
  526.0 3.7 copy.125
  529.6 6.9 %all-to-all-start.3 = ((bf16[2,32,17,1024]{3,0,2,1:T(2,128)(2,1)}), bf16[2,32,17,1024]{3,0,2,1:T(2,128)(2,1)}, u32[]{:S(2)}, u32[]{:S(2)}) async-start(bf16[2,32,17,1024]{3,0,2,1:T(2,128)(2,1)} %copy.125), calls=%async_computation.3 | async-start | bytes 4456448 | tf_op jit(solution)/shard_map/all_to_all | solution.py:127
  537.6 7.1 %gather_fusion.2 = s32[1024]{0:T(1024)S(1)} fusion(s32[128,64]{1,0:T(8,128)S(1)} %sub.31, s32[1024]{0:T(1024)S(1)} %reshape.148), kind=kCustom, calls=%fused_computation.2 | custom fusion | bytes 16384 | tf_op jit(solution)/shard_map/jit(take_along_axis)/gather | solution.py:45
  546.9 6.2 %gather_fusion.1 = f32[1024]{0:T(1024)S(1)} fusion(f32[1088]{0:T(1024)S(1)} %convolution_reduce_fusion, s32[1024]{0:T(1024)S(1)} %broadcast_clamp_fusion), kind=kCustom, calls=%fused_computation.1 | custom fusion | bytes 12288 | tf_op jit(solution)/shard_map/jit(_take)/gather | solution.py:107
  554.5 34.5 %all-to-all-done.3 = bf16[2,32,17,1024]{3,0,2,1:T(2,128)(2,1)} async-done(((bf16[2,32,17,1024]{3,0,2,1:T(2,128)(2,1)}), bf16[2,32,17,1024]{3,0,2,1:T(2,128)(2,1)}, u32[]{:S(2)}, u32[]{:S(2)}) %all-to-all-start.3) | async-done | bytes 2228256 | tf_op jit(solution)/shard_map/all_to_all | solution.py:127
  589.0 2.5 copy.126
  593.8 2.9 fusion.18
  (86 shorter events, 34.4 us)
Async XLA Ops:
  7.2 50.0 %all-gather.6.cloned.1.call-start = ((), (), s32[]{:S(2)}) async-start(), calls=%async_computation.4 | async-start | bytes 1671168 | tf_op jit(solution)/shard_map/all_gather | solution.py:36
  7.9 93.3 %all-gather.8.cloned.1.call-start = ((), (), s32[]{:S(2)}) async-start(), calls=%async_computation.5 | async-start | bytes 1671168 | tf_op jit(solution)/shard_map/all_gather | solution.py:37
  14.7 82.3 %all-to-all-start = ((bf16[64,1,17,1024]{3,2,1,0:T(8,128)(2,1)}), bf16[64,1,17,1024]{3,2,1,0:T(8,128)(2,1)S(1)}, u32[]{:S(2)}, u32[]{:S(2)}) async-start(bf16[64,1,17,1024]{3,2,1,0:T(8,128)(2,1)} %copy.118), calls=%async_computation | async-start | bytes 6291456 | tf_op jit(solution)/shard_map/all_to_all | solution.py:57
  24.7 118.0 %all-gather.10.cloned.1.call-start = ((), (), s32[]{:S(2)}) async-start(), calls=%async_computation.6 | async-start | bytes 1671168 | tf_op jit(solution)/shard_map/all_gather | solution.py:38
  150.2 10.2 %copy-start.3 = (s32[128,8]{0,1:T(8,128)S(1)}, s32[128,8]{0,1:T(8,128)}, u32[]{:S(2)}) copy-start(s32[128,8]{0,1:T(8,128)} %param.8) | copy-start | bytes 12292
  150.2 10.2 %copy-start.7 = (f32[128,8]{0,1:T(8,128)S(1)}, f32[128,8]{0,1:T(8,128)}, u32[]{:S(2)}) copy-start(f32[128,8]{0,1:T(8,128)} %param.9) | copy-start | bytes 12292
  150.2 10.7 %copy-start = (bf16[128,1024]{1,0:T(8,128)(2,1)S(1)}, bf16[128,1024]{1,0:T(8,128)(2,1)}, u32[]{:S(2)}) copy-start(bf16[128,1024]{1,0:T(8,128)(2,1)} %param.7) | copy-start | bytes 786436
  150.2 63.2 %all-to-all-start.1 = ((bf16[2,32,17,1024]{3,0,2,1:T(2,128)(2,1)}), bf16[2,32,17,1024]{3,0,2,1:T(2,128)(2,1)S(1)}, u32[]{:S(2)}, u32[]{:S(2)}) async-start(bf16[2,32,17,1024]{3,0,2,1:T(2,128)(2,1)} %copy.121), calls=%async_computation.1 | async-start | bytes 4456448 | tf_op jit(solution)/shard_map/all_to_all | solution.py:62
  160.2 167.7 %all-gather.12.cloned.1.call-start = ((), (), s32[]{:S(2)}) async-start(), calls=%async_computation.7 | async-start | bytes 1050624 | tf_op jit(solution)/shard_map/all_gather | solution.py:71
  160.8 55.3 %copy-start.2 = (f32[64,17]{1,0:T(8,128)}, f32[64,17]{1,0:T(8,128)S(1)}, u32[]{:S(2)}) copy-start(f32[64,17]{1,0:T(8,128)S(1)} %select_reduce_fusion) | copy-start | bytes 13060
  219.1 2.9 copy-start.5
  434.3 1.8 copy-start.6
  438.4 1.3 copy-start.4
  441.6 79.0 %copy-start.10 = (bf16[2,384,1024]{2,1,0:T(8,128)(2,1)S(1)}, bf16[2,384,1024]{2,1,0:T(8,128)(2,1)}, u32[]{:S(2)}) copy-start(bf16[2,384,1024]{2,1,0:T(8,128)(2,1)} %all-gather.10.cloned.1.call-done) | copy-start | bytes 4718596
  520.6 1.8 copy-start.8
  520.6 1.9 copy-start.11
  520.6 2.4 copy-start.12
  523.0 1.5 copy-start.9
  529.6 59.3 %all-to-all-start.3 = ((bf16[2,32,17,1024]{3,0,2,1:T(2,128)(2,1)}), bf16[2,32,17,1024]{3,0,2,1:T(2,128)(2,1)}, u32[]{:S(2)}, u32[]{:S(2)}) async-start(bf16[2,32,17,1024]{3,0,2,1:T(2,128)(2,1)} %copy.125), calls=%async_computation.3 | async-start | bytes 4456448 | tf_op jit(solution)/shard_map/all_to_all | solution.py:127
  591.5 2.3 copy-start.1
Sparse Core Ops, SparseCore 0:
  10.1 46.9 all-gather.5
  59.3 40.5 all-gather.7
  102.1 40.6 all-gather.9
  222.1 105.7 all-gather.11
where the time goes:
time: 605 us; the launch traced here: 604 us
  waiting for transfers between devices  301 us (50%)
  blocking collectives  177 us (29%)
  local copies, waits for them, and re-layouts  44.9 us (7%)
  starting transfers between devices  27.3 us (5%)
  matrix products  26.4 us (4%)
  between operations  18 us (3%)
  other arithmetic  10.6 us (2%)
    all_gather x1, waiting for transfers between devices, on_device(): gathered = lax.all_gather(embedding, ('dp', 'expert'), axis=0, tiled=True)  103 us
    unnamed x1, blocking collectives  97.6 us
    all_to_all x1, blocking collectives, on_device(): lax.all_to_all(out_grad, 'expert', split_axis=0, concat_axis=1, tiled=True)  79 us
    all_to_all x1, waiting for transfers between devices, on_device(): lax.all_to_all(out_here, 'expert', split_axis=1, concat_axis=0, tiled=True)  52.4 us
    all_to_all x1, waiting for transfers between devices, on_device(): lax.all_to_all(outgoing, 'expert', split_axis=0, concat_axis=1, tiled=True)  39.8 us
    all_gather x1, waiting for transfers between devices, on_device(): lax.all_gather(w_down, 'dp', axis=1, tiled=True)  37.3 us
    all_to_all x1, waiting for transfers between devices, on_device(): lax.all_to_all(route_here, 'expert', split_axis=1, concat_axis=0, tiled=T...  34.5 us
    all_gather x1, waiting for transfers between devices, on_device(): lax.all_gather(w_gate, 'dp', axis=1, tiled=True)  31.7 us
  transfers between devices with their start and end apart: 7, of which 6 were waited for; matrix products, arithmetic and copies ran while one was open for 6% of the time, Pallas kernels for 0%

commit v1 on v0

--- a/solution.py
+++ b/solution.py
@@ -68,7 +68,12 @@
     pooled = jnp.mean(tokens.astype(jnp.float32), axis=0) + weighted_sum / tok_rows
     inv_rms = lax.rsqrt(jnp.mean(pooled * pooled) + 1e-06)
     embedding = (pooled * inv_rms).astype(jnp.bfloat16)[None, :]
-    gathered = lax.all_gather(embedding, ("dp", "expert"), axis=0, tiled=True)
+    gathered = jnp.concatenate(
+        lax.all_to_all(
+            jnp.stack([embedding] * lax.axis_size(("dp", "expert"))), ("dp", "expert"), 0, 0
+        ),
+        axis=0,
+    )
     batch_size = gathered.shape[0]
     own_index = lax.axis_index(("dp", "expert"))
     batch_iota = jnp.arange(batch_size, dtype=jnp.int32)

time: 605 us -> 564 us (0.932); the launches traced: 604 us -> 556 us
  waiting for transfers between devices: 301 us -> 228 us
  starting transfers between devices: 27.3 us -> 38.9 us
  other arithmetic: 10.6 us -> 18.8 us
  local copies, waits for them, and re-layouts: 44.9 us -> 52.3 us
    all_gather x1 -> x0, waiting for transfers between devices: 103 us -> none  [on_device(): gathered = lax.all_gather(embedding, ('dp', 'expert'), axis=0, tiled=True)]
    all_to_all x0 -> x1, waiting for transfers between devices: none -> 29.9 us  [on_device(): lax.all_to_all(jnp.stack([embedding] * lax.axis_size(('dp', 'expert'))),...]
    all_to_all x0 -> x1, starting transfers between devices: none -> 11.2 us  [on_device(): lax.all_to_all(jnp.stack([embedding] * lax.axis_size(('dp', 'expert'))),...]
    another operation x0 -> x1, other arithmetic: none -> 8.03 us  [on_device(): jnp.stack([embedding] * lax.axis_size(('dp', 'expert')))]
    unnamed x28 -> x33, local copies, waits for them, and re-layouts: 2.64 us -> 9.58 us
where the time goes in v1:
time: 564 us; the launch traced here: 556 us
  waiting for transfers between devices  228 us (40%)
  blocking collectives  174 us (31%)
  local copies, waits for them, and re-layouts  52.3 us (9%)
  starting transfers between devices  38.9 us (7%)
  matrix products  25.7 us (5%)
  other arithmetic  18.8 us (3%)
  between operations  18.1 us (3%)
    unnamed x1, blocking collectives  93.5 us
    all_to_all x1, blocking collectives, on_device(): lax.all_to_all(out_grad, 'expert', split_axis=0, concat_axis=1, tiled=True)  80.4 us
    all_to_all x1, waiting for transfers between devices, on_device(): lax.all_to_all(out_here, 'expert', split_axis=1, concat_axis=0, tiled=True)  52.5 us
    all_to_all x1, waiting for transfers between devices, on_device(): lax.all_to_all(outgoing, 'expert', split_axis=0, concat_axis=1, tiled=True)  39.7 us
    all_gather x1, waiting for transfers between devices, on_device(): lax.all_gather(w_down, 'dp', axis=1, tiled=True)  37.4 us
    all_to_all x1, waiting for transfers between devices, on_device(): lax.all_to_all(route_here, 'expert', split_axis=1, concat_axis=0, tiled=T...  34.6 us
    all_gather x1, waiting for transfers between devices, on_device(): lax.all_gather(w_gate, 'dp', axis=1, tiled=True)  31.7 us
    all_to_all x1, waiting for transfers between devices, on_device(): lax.all_to_all(jnp.stack([embedding] * lax.axis_size(('dp', 'expert'))),...  29.9 us
  transfers between devices with their start and end apart: 7, of which 6 were waited for; matrix products, arithmetic and copies ran while one was open for 6% of the time, Pallas kernels for 0%

profile of v1, /device:TPU:16, one launch (start us, length us, event | category | flops | bytes accessed | tf_op | source)
XLA Modules:
  0.0 555.5 jit_solution(12222734986261897400)
XLA Ops:
  11.6 3.0 copy.118
  14.6 10.1 %all-to-all-start = ((bf16[64,1,17,1024]{3,2,1,0:T(8,128)(2,1)}), bf16[64,1,17,1024]{3,2,1,0:T(8,128)(2,1)S(1)}, u32[]{:S(2)}, u32[]{:S(2)}) async-start(bf16[64,1,17,1024]{3,2,1,0:T(8,128)(2,1)} %copy.118), calls=%async_computation | async-start | bytes 6291456 | tf_op jit(solution)/shard_map/all_to_all | solution.py:57
  25.4 31.7 %all-gather.4.cloned.1.call-done = bf16[2,1024,384]{2,1,0:T(8,128)(2,1)} async-done(((bf16[2,64,384]{2,1,0:T(8,128)(2,1)}), bf16[2,1024,384]{2,1,0:T(8,128)(2,1)}) %all-gather.4.cloned.1.call-update) | async-done | bytes 1572880 | tf_op jit(solution)/shard_map/all_gather | solution.py:36
  57.1 39.7 %all-to-all-done = bf16[64,1,17,1024]{3,2,1,0:T(8,128)(2,1)S(1)} async-done(((bf16[64,1,17,1024]{3,2,1,0:T(8,128)(2,1)}), bf16[64,1,17,1024]{3,2,1,0:T(8,128)(2,1)S(1)}, u32[]{:S(2)}, u32[]{:S(2)}) %all-to-all-start) | async-done | bytes 2228256 | tf_op jit(solution)/shard_map/all_to_all | solution.py:57
  96.9 4.2 fusion.5
  101.1 4.2 fusion.3
  105.4 37.4 %all-gather.8.cloned.1.call-done = bf16[2,384,1024]{2,1,0:T(8,128)(2,1)} async-done(((bf16[2,24,1024]{2,1,0:T(8,128)(2,1)}), bf16[2,384,1024]{2,1,0:T(8,128)(2,1)}) %all-gather.8.cloned.1.call-update) | async-done | bytes 1572880 | tf_op jit(solution)/shard_map/all_gather | solution.py:38
  142.7 3.8 convolution_convert_fusion
  146.5 3.7 copy.121
  150.2 10.5 %all-to-all-start.1 = ((bf16[2,32,17,1024]{3,0,2,1:T(2,128)(2,1)}), bf16[2,32,17,1024]{3,0,2,1:T(2,128)(2,1)S(1)}, u32[]{:S(2)}, u32[]{:S(2)}) async-start(bf16[2,32,17,1024]{3,0,2,1:T(2,128)(2,1)} %copy.121), calls=%async_computation.1 | async-start | bytes 4456448 | tf_op jit(solution)/shard_map/all_to_all | solution.py:62
  161.3 52.5 %all-to-all-done.1 = bf16[2,32,17,1024]{3,0,2,1:T(2,128)(2,1)S(1)} async-done(((bf16[2,32,17,1024]{3,0,2,1:T(2,128)(2,1)}), bf16[2,32,17,1024]{3,0,2,1:T(2,128)(2,1)S(1)}, u32[]{:S(2)}, u32[]{:S(2)}) %all-to-all-start.1) | async-done | bytes 2228256 | tf_op jit(solution)/shard_map/all_to_all | solution.py:62
  216.4 3.0 reshape.133
  224.7 8.0 %reduce.4 = bf16[512,1024]{1,0:T(8,128)(2,1)S(1)} reduce(bf16[512,1,1024]{2,1,0:T(2,128)(2,1)} %stack.3, bf16[]{:T(256)} %broadcast.162), dimensions={1}, to_apply=%stack.3.reduce_sub_computation | reduce | bytes 2097154 | tf_op jit(solution)/shard_map/stack | solution.py:73
  234.3 11.2 %all-to-all-start.2 = ((bf16[512,2,512]{2,1,0:T(2,128)(2,1)}), bf16[512,2,512]{2,1,0:T(2,128)(2,1)S(1)}, u32[]{:S(2)}, u32[]{:S(2)}) async-start(bf16[512,2,512]{2,1,0:T(2,128)(2,1)} %reshape.187), calls=%async_computation.2 | async-start | bytes 2097152 | tf_op jit(solution)/shard_map/all_to_all | solution.py:72
  247.9 29.9 %all-to-all-done.2 = bf16[512,2,512]{2,1,0:T(2,128)(2,1)S(1)} async-done(((bf16[512,2,512]{2,1,0:T(2,128)(2,1)}), bf16[512,2,512]{2,1,0:T(2,128)(2,1)S(1)}, u32[]{:S(2)}, u32[]{:S(2)}) %all-to-all-start.2) | async-done | bytes 1048608 | tf_op jit(solution)/shard_map/all_to_all | solution.py:72
  277.8 3.3 reshape.188
  286.7 93.5 %all-reduce = f32[512]{0:T(512)} all-reduce(f32[512]{0:T(512)} %dynamic-update-slice), channel_id=1, replica_groups=mesh['dp'=16,'expert'=32] {'dp','expert'}, use_global_device_ids=true, to_apply=%add | all-reduce | flops 512 | bytes 4096
  380.3 2.9 gather_fusion
  391.1 80.4 %all_to_all.71 = bf16[64,1,17,1024]{3,2,1,0:T(8,128)(2,1)S(1)} all-to-all(bf16[64,1,17,1024]{3,2,1,0:T(8,128)(2,1)S(1)} %multiply_convert_fusion), channel_id=1, replica_groups=mesh['dp'=16,'expert'=32] {'expert'}, dimensions={0} | all-to-all | bytes 4456448 | tf_op jit(solution)/shard_map/all_to_all | solution.py:118
  476.9 3.7 copy.125
  480.6 7.0 %all-to-all-start.4 = ((bf16[2,32,17,1024]{3,0,2,1:T(2,128)(2,1)}), bf16[2,32,17,1024]{3,0,2,1:T(2,128)(2,1)}, u32[]{:S(2)}, u32[]{:S(2)}) async-start(bf16[2,32,17,1024]{3,0,2,1:T(2,128)(2,1)} %copy.125), calls=%async_computation.4 | async-start | bytes 4456448 | tf_op jit(solution)/shard_map/all_to_all | solution.py:132
  488.5 7.1 %gather_fusion.2 = s32[1024]{0:T(1024)S(1)} fusion(s32[128,64]{1,0:T(8,128)S(1)} %sub.31, s32[1024]{0:T(1024)S(1)} %reshape.154), kind=kCustom, calls=%fused_computation.2 | custom fusion | bytes 16384 | tf_op jit(solution)/shard_map/jit(take_along_axis)/gather | solution.py:45
  497.8 6.2 %gather_fusion.1 = f32[1024]{0:T(1024)S(1)} fusion(f32[1088]{0:T(1024)S(1)} %convolution_reduce_fusion, s32[1024]{0:T(1024)S(1)} %broadcast_clamp_fusion), kind=kCustom, calls=%fused_computation.1 | custom fusion | bytes 12288 | tf_op jit(solution)/shard_map/jit(_take)/gather | solution.py:112
  505.3 34.6 %all-to-all-done.4 = bf16[2,32,17,1024]{3,0,2,1:T(2,128)(2,1)} async-done(((bf16[2,32,17,1024]{3,0,2,1:T(2,128)(2,1)}), bf16[2,32,17,1024]{3,0,2,1:T(2,128)(2,1)}, u32[]{:S(2)}, u32[]{:S(2)}) %all-to-all-start.4) | async-done | bytes 2228256 | tf_op jit(solution)/shard_map/all_to_all | solution.py:132
  (92 shorter events, 45.9 us)
Async XLA Ops:
  7.2 50.0 %all-gather.4.cloned.1.call-start = ((), (), s32[]{:S(2)}) async-start(), calls=%async_computation.5 | async-start | bytes 1671168 | tf_op jit(solution)/shard_map/all_gather | solution.py:36
  7.9 93.2 %all-gather.6.cloned.1.call-start = ((), (), s32[]{:S(2)}) async-start(), calls=%async_computation.6 | async-start | bytes 1671168 | tf_op jit(solution)/shard_map/all_gather | solution.py:37
  14.6 82.3 %all-to-all-start = ((bf16[64,1,17,1024]{3,2,1,0:T(8,128)(2,1)}), bf16[64,1,17,1024]{3,2,1,0:T(8,128)(2,1)S(1)}, u32[]{:S(2)}, u32[]{:S(2)}) async-start(bf16[64,1,17,1024]{3,2,1,0:T(8,128)(2,1)} %copy.118), calls=%async_computation | async-start | bytes 6291456 | tf_op jit(solution)/shard_map/all_to_all | solution.py:57
  24.7 118.0 %all-gather.8.cloned.1.call-start = ((), (), s32[]{:S(2)}) async-start(), calls=%async_computation.7 | async-start | bytes 1671168 | tf_op jit(solution)/shard_map/all_gather | solution.py:38
  150.2 10.5 %copy-start.3 = (s32[128,8]{0,1:T(8,128)S(1)}, s32[128,8]{0,1:T(8,128)}, u32[]{:S(2)}) copy-start(s32[128,8]{0,1:T(8,128)} %param.8) | copy-start | bytes 12292
  150.2 10.6 %copy-start.8 = (f32[128,8]{0,1:T(8,128)S(1)}, f32[128,8]{0,1:T(8,128)}, u32[]{:S(2)}) copy-start(f32[128,8]{0,1:T(8,128)} %param.9) | copy-start | bytes 12292
  150.2 11.1 %copy-start = (bf16[128,1024]{1,0:T(8,128)(2,1)S(1)}, bf16[128,1024]{1,0:T(8,128)(2,1)}, u32[]{:S(2)}) copy-start(bf16[128,1024]{1,0:T(8,128)(2,1)} %param.7) | copy-start | bytes 786436
  150.2 63.6 %all-to-all-start.1 = ((bf16[2,32,17,1024]{3,0,2,1:T(2,128)(2,1)}), bf16[2,32,17,1024]{3,0,2,1:T(2,128)(2,1)S(1)}, u32[]{:S(2)}, u32[]{:S(2)}) async-start(bf16[2,32,17,1024]{3,0,2,1:T(2,128)(2,1)} %copy.121), calls=%async_computation.1 | async-start | bytes 4456448 | tf_op jit(solution)/shard_map/all_to_all | solution.py:62
  161.1 55.3 %copy-start.2 = (f32[64,17]{1,0:T(8,128)}, f32[64,17]{1,0:T(8,128)S(1)}, u32[]{:S(2)}) copy-start(f32[64,17]{1,0:T(8,128)S(1)} %select_reduce_fusion) | copy-start | bytes 13060
  232.7 12.8 %copy-start.5 = (s32[512]{0:T(512)S(1)}, s32[512]{0:T(512)}, u32[]{:S(2)}) copy-start(s32[512]{0:T(512)} %param.13) | copy-start | bytes 6148
  234.3 43.5 %all-to-all-start.2 = ((bf16[512,2,512]{2,1,0:T(2,128)(2,1)}), bf16[512,2,512]{2,1,0:T(2,128)(2,1)S(1)}, u32[]{:S(2)}, u32[]{:S(2)}) async-start(bf16[512,2,512]{2,1,0:T(2,128)(2,1)} %reshape.187), calls=%async_computation.2 | async-start | bytes 2097152 | tf_op jit(solution)/shard_map/all_to_all | solution.py:72
  281.1 2.0 copy-start.6
  383.2 2.5 copy-start.7
  388.0 1.3 copy-start.4
  391.1 80.4 %copy-start.11 = (bf16[2,384,1024]{2,1,0:T(8,128)(2,1)S(1)}, bf16[2,384,1024]{2,1,0:T(8,128)(2,1)}, u32[]{:S(2)}) copy-start(bf16[2,384,1024]{2,1,0:T(8,128)(2,1)} %all-gather.8.cloned.1.call-done) | copy-start | bytes 4718596
  471.5 1.8 copy-start.9
  471.5 1.9 copy-start.12
  471.5 2.4 copy-start.13
  474.0 1.5 copy-start.10
  480.6 59.4 %all-to-all-start.4 = ((bf16[2,32,17,1024]{3,0,2,1:T(2,128)(2,1)}), bf16[2,32,17,1024]{3,0,2,1:T(2,128)(2,1)}, u32[]{:S(2)}, u32[]{:S(2)}) async-start(bf16[2,32,17,1024]{3,0,2,1:T(2,128)(2,1)} %copy.125), calls=%async_computation.4 | async-start | bytes 4456448 | tf_op jit(solution)/shard_map/all_to_all | solution.py:132
  542.5 2.3 copy-start.1
Sparse Core Ops, SparseCore 0:
  10.1 46.9 all-gather.3
  59.3 40.5 all-gather.5
  102.1 40.6 all-gather.7
